TPU v7x, 128 devices: a whole 4x4x4 slice. The times are simulated.
128 devices in a mesh: depth: 4 (over z_lo, core), lat: 32 (over y, z_hi, x).
Axes of the slice: x: 4, y: 4, z: 4 (z_hi: 2, z_lo: 2; z = z_hi * 2 + z_lo), core: 2. Of those that a mesh axis runs over, the one named last changes fastest.
Arguments:
- temp_old: float32 [32, 32, 256, 128], P('depth', 'lat'), may hold values from 0 to 2.5
- material: int32 [32, 32, 256, 128], P('depth', 'lat'), may hold values from 0 to 7
- conduct_table: float32 [8], replicated, may hold values from 0.3 to 3
- capacity_table: float32 [8], replicated, may hold values from 0.5 to 2
- dyn_power: float32 [4, 32, 256, 128], P('depth', 'lat'), may hold values from 0.2 to 4
- leak_ref: float32 [4, 32, 256, 128], P('depth', 'lat'), may hold values from 0.05 to 1
- die_layer: int32 [4], replicated, may hold values from 0 to 31, as said below
Outputs:
- temp_new: float32 [32, 32, 256, 128], P('depth', 'lat')
- die_power: float32 [4, 32, 256, 128], P('depth', 'lat')
Inputs may be any that keep to these rules, and one draw needn't show every extreme that they name: `die_layer`: the 4 entries name different layers of the grid; one die lies on layer 0 and one on the top layer.
All inputs are finite; a program needn't handle non-finite values.
Results may differ from a plain program's by a relative error of at most 0.000059.
Values sent between devices are 32-bit elements; how exact they have to be, the bound alone decides.
No kernel may reach another device: no remote copies, remote signals or barrier semaphores. Data moves between devices by JAX's collectives and lax.ppermute only.
A program may use at most 128 MiB of HBM per device.

v0:
```python
import functools

import jax
import jax.numpy as jnp
from jax import lax
from jax.experimental import pallas as pl
from jax.experimental.pallas import tpu as pltpu
from jax.sharding import PartitionSpec as P


SWEEPS = 6
HALO = SWEEPS
PAD_Y = 8

COND_SLOPE = 0.15
LEAK_SLOPE = 0.5
SINK_CONDUCT = 2.0

INTERPRET = False


def from_behind(block, axis, distance):
    devices = range(lax.axis_size(axis))
    route = [(i - distance, i) for i in devices if i - distance in devices]
    return lax.ppermute(block, axis, route)


def harm(a, b):
    summed = a + b
    return 2.0 * a * b / jnp.where(summed > 0, summed, 1.0)


def material_bits(material):
    hi = material >= 4.0
    rest = material - jnp.where(hi, 4.0, 0.0)
    mid = rest >= 2.0
    lo = (rest - jnp.where(mid, 2.0, 0.0)) >= 1.0
    return hi, mid, lo


def lookup(table_ref, bits):
    hi, mid, lo = bits
    t = [table_ref[i] for i in range(8)]
    low = jnp.where(mid, jnp.where(lo, t[3], t[2]), jnp.where(lo, t[1], t[0]))
    high = jnp.where(mid, jnp.where(lo, t[7], t[6]), jnp.where(lo, t[5], t[4]))
    return jnp.where(hi, high, low)


def sweep_kernel(nz, ny_total, local_depth, strip,
                 sc_ref, ctab_ref, htab_ref, tc_ref, mc_ref, tb_ref, mb_ref, ta_ref, ma_ref,
                 ylo_ref, yhi_ref, cb_ref, ca_ref, d0_ref, d1_ref, d2_ref, d3_ref,
                 out_ref, t_s, cond_s, rhs_s, inv_s, gz_s, gx_s, gxl_s, gy_s, gyu_s):
    ze = t_s.shape[1]
    ye = t_s.shape[2]
    xe = t_s.shape[3]
    g = sc_ref[0]
    s = sc_ref[1]
    z0 = g * local_depth - HALO
    row = lax.broadcasted_iota(jnp.int32, (ye, xe), 0)
    lane = lax.broadcasted_iota(jnp.int32, (ye, xe), 1)
    yg = s * strip + row - PAD_Y
    yvalid = (yg >= 0) & (yg < ny_total) & (row >= PAD_Y - HALO) & (row < PAD_Y + strip + HALO)
    top = PAD_Y + strip + HALO
    zlo = jnp.zeros((PAD_Y - HALO, xe), jnp.float32)
    zhi = jnp.zeros((ye - top, xe), jnp.float32)

    def put(dst, centre, lo, hi):
        dst[PAD_Y - HALO:PAD_Y] = lo
        dst[PAD_Y:PAD_Y + strip] = centre
        dst[PAD_Y + strip:top] = hi
        dst[0:PAD_Y - HALO] = zlo
        dst[top:ye] = zhi

    def tables(l, temp_raw, mat_raw, t_lo, t_hi, m_lo, m_hi):
        put(t_s.at[0, l], temp_raw.T, t_lo, t_hi)
        put(cond_s.at[l], mat_raw.T.astype(jnp.float32), m_lo, m_hi)
        temp = t_s[0, l]
        mat = cond_s[l]
        zg = z0 + l
        valid = yvalid & (zg >= 0) & (zg < nz)
        bits = material_bits(mat)
        cval = lookup(ctab_ref, bits)
        hval = lookup(htab_ref, bits)
        cond = jnp.where(valid, cval * jnp.exp(-COND_SLOPE * temp), 0.0)
        cond_s[l] = cond
        inv_s[l] = hval
        rhs_s[l] = hval * temp

    def below(i, c):
        tables(i, tb_ref[i], mb_ref[i], cb_ref[0, i, :HALO], cb_ref[0, i, HALO:],
               cb_ref[1, i, :HALO], cb_ref[1, i, HALO:])
        return c

    def centre(i, c):
        tables(HALO + i, tc_ref[i], mc_ref[i], ylo_ref[i], yhi_ref[i],
               ylo_ref[local_depth + i], yhi_ref[local_depth + i])
        return c

    def above(i, c):
        tables(HALO + local_depth + i, ta_ref[i], ma_ref[i], ca_ref[0, i, :HALO], ca_ref[0, i, HALO:],
               ca_ref[1, i, :HALO], ca_ref[1, i, HALO:])
        return c

    lax.fori_loop(0, HALO, below, 0)
    lax.fori_loop(0, local_depth, centre, 0)
    lax.fori_loop(0, HALO, above, 0)

    slots = (d0_ref, d1_ref, d2_ref, d3_ref)
    dies = len(slots)
    for o in range(dies):
        rel = sc_ref[2 + (g + dies - o) % dies] - z0
        relc = jnp.clip(rel, 0, ze - 1)

        @pl.when((rel >= 0) & (rel < ze))
        def _():
            rhs_s[relc] = inv_s[relc] * t_s[0, relc] + slots[o][...]

    def faces_z(l, c):
        gz_s[l] = harm(cond_s[l], cond_s[l + 1])
        return c

    lax.fori_loop(0, ze - 1, faces_z, 0)
    gz_s[ze - 1] = jnp.zeros((ye, xe), jnp.float32)

    def faces(l, c):
        cc = cond_s[l]
        gx = harm(cc, pltpu.roll(cc, xe - 1, 1))
        gx = jnp.where(lane == xe - 1, 0.0, gx)
        gy = harm(cc, pltpu.roll(cc, ye - 1, 0))
        gy = jnp.where(row == ye - 1, 0.0, gy)
        gxl = pltpu.roll(gx, 1, 1)
        gyu = pltpu.roll(gy, 1, 0)
        gx_s[l] = gx
        gxl_s[l] = gxl
        gy_s[l] = gy
        gyu_s[l] = gyu
        lm = jnp.maximum(l - 1, 0)
        gzm = jnp.where(l > 0, gz_s[lm], 0.0)
        sink = jnp.where(z0 + l == 0, SINK_CONDUCT, 0.0)
        diag = inv_s[l] + (gz_s[l] + gzm + gx + gxl + gy + gyu) + sink
        inv_s[l] = 1.0 / diag
        return c

    lax.fori_loop(0, ze, faces, 0)

    def relax(src, l):
        t = t_s[src, l]
        coupled = (gz_s[l] * t_s[src, l + 1] + gz_s[l - 1] * t_s[src, l - 1]
                   + gx_s[l] * pltpu.roll(t, xe - 1, 1) + gxl_s[l] * pltpu.roll(t, 1, 1)
                   + gy_s[l] * pltpu.roll(t, ye - 1, 0) + gyu_s[l] * pltpu.roll(t, 1, 0))
        return (rhs_s[l] + coupled) * inv_s[l]

    for k in range(1, SWEEPS):
        src, dst = (k - 1) % 2, k % 2

        def body(l, c, src=src, dst=dst):
            t_s[dst, l] = relax(src, l)
            return c

        lax.fori_loop(k, ze - k, body, 0)

    last = (SWEEPS - 1) % 2

    def final(i, c):
        new = relax(last, HALO + i)
        out_ref[i] = new[PAD_Y:PAD_Y + strip].T
        return c

    lax.fori_loop(0, local_depth, final, 0)


def local_body(temp_old, material, conduct_table, capacity_table, dyn_power, leak_ref, die_layer):
    temp_start = temp_old[:, 0]
    cells_mat = material[:, 0]
    local_depth, nx, strip = temp_start.shape
    depth_n = lax.axis_size("depth")
    lat_n = lax.axis_size("lat")
    dies = dyn_power.shape[0] * depth_n
    nz = local_depth * depth_n
    g = lax.axis_index("depth")
    s = lax.axis_index("lat")
    first_layer = g * local_depth
    ye = PAD_Y + strip + HALO + (-(PAD_Y + strip + HALO)) % 8

    tb = from_behind(temp_start[local_depth - HALO:], "depth", 1)
    mb = from_behind(cells_mat[local_depth - HALO:], "depth", 1)
    ta = from_behind(temp_start[:HALO], "depth", -1)
    ma = from_behind(cells_mat[:HALO], "depth", -1)

    def cols(sl):
        parts = [temp_start[:, :, sl], cells_mat[:, :, sl].astype(jnp.float32),
                 dyn_power[:, 0, :, sl], leak_ref[:, 0, :, sl]]
        return jnp.transpose(jnp.concatenate(parts), (0, 2, 1))

    nf = 2 * local_depth + 2
    ylo = from_behind(cols(slice(strip - HALO, strip)), "lat", 1)
    yhi = from_behind(cols(slice(0, HALO)), "lat", -1)

    def widen(centre, lo, hi):
        return jnp.concatenate([jnp.zeros((PAD_Y - HALO, nx), jnp.float32), lo, centre, hi,
                                jnp.zeros((ye - (PAD_Y + strip + HALO), nx), jnp.float32)])

    side = jnp.concatenate([ylo[:2 * local_depth].reshape(2, local_depth, HALO, nx),
                            yhi[:2 * local_depth].reshape(2, local_depth, HALO, nx)], axis=2)
    corner_of = {1: side[:, local_depth - HALO:], dies - 1: side[:, :HALO]}

    def pick(die):
        at = die_layer[die] - first_layer
        atc = jnp.clip(at, 0, local_depth - 1)
        layer = widen(lax.dynamic_index_in_dim(temp_start, atc, 0, keepdims=False).T,
                      lax.dynamic_index_in_dim(ylo, atc, 0, keepdims=False),
                      lax.dynamic_index_in_dim(yhi, atc, 0, keepdims=False))
        return jnp.where((at >= 0) & (at < local_depth), layer, 0.0)

    die_temp = pick(g)
    got_corners = {}
    for o in range(1, dies):
        route = [(i, (i + o) % depth_n) for i in range(depth_n)]
        sent = pick((g + o) % dies)
        if o in corner_of:
            sent = jnp.concatenate([sent, corner_of[o].reshape(-1, nx)])
        got = lax.ppermute(sent, "depth", route)
        die_temp = die_temp + got[:ye]
        if o in corner_of:
            got_corners[o] = got[ye:].reshape(2, HALO, 2 * HALO, nx)
    cb, ca = got_corners[1], got_corners[dies - 1]
    dyn_w = widen(dyn_power[0, 0].T, ylo[nf - 2], yhi[nf - 2])
    leak_w = widen(leak_ref[0, 0].T, ylo[nf - 1], yhi[nf - 1])
    power_w = dyn_w + leak_w * jnp.exp(LEAK_SLOPE * die_temp)
    die_power = power_w[PAD_Y:PAD_Y + strip].T[None]

    slots = [power_w]
    for o in range(1, dies):
        route = [(i, (i + o) % depth_n) for i in range(depth_n)]
        slots.append(lax.ppermute(power_w, "depth", route))

    sc = jnp.concatenate([jnp.stack([g, s]).astype(jnp.int32), die_layer.astype(jnp.int32)])
    ze = local_depth + 2 * HALO
    smem = pl.BlockSpec(memory_space=pltpu.MemorySpace.SMEM)
    vmem = pl.BlockSpec(memory_space=pltpu.MemorySpace.VMEM)
    full = (ze, ye, nx)
    kern = functools.partial(sweep_kernel, nz, strip * lat_n, local_depth, strip)
    out = pl.pallas_call(
        kern,
        out_shape=jax.ShapeDtypeStruct((local_depth, nx, strip), jnp.float32),
        in_specs=[smem] * 3 + [vmem] * 14,
        out_specs=vmem,
        scratch_shapes=([pltpu.VMEM((2,) + full, jnp.float32)] + [pltpu.VMEM(full, jnp.float32)] * 8),
        compiler_params=pltpu.CompilerParams(vmem_limit_bytes=60 * 1024 * 1024),
        interpret=INTERPRET,
    )(sc, conduct_table, capacity_table, temp_start, cells_mat, tb, mb, ta, ma, ylo, yhi, cb, ca, *slots)
    return (out[:, None], die_power[:, None])


def solution(mesh):
    return jax.shard_map(
        local_body,
        mesh=mesh,
        in_specs=(
            P("depth", "lat", None, None),
            P("depth", "lat", None, None),
            P(),
            P(),
            P("depth", "lat", None, None),
            P("depth", "lat", None, None),
            P(),
        ),
        out_specs=(P("depth", "lat", None, None), P("depth", "lat", None, None)),
        check_vma=False,
    )
```

profile of v0, /device:TPU:70, one launch (start us, length us, event | category | flops | bytes accessed | tf_op | source)
XLA Modules:
  0.0 106.1 jit_solution(4389549167970339474)
XLA Ops:
  0.6 1.0 copy.35
  1.8 1.6 %copy.29 = f32[8,1,256,128]{2,3,0,1:T(8,128)S(1)} copy(f32[8,1,256,128]{3,2,1,0:T(8,128)} %param.7) | data formatting | bytes 2097152 | tf_op args[0]
  4.5 0.8 copy-done.10
  6.0 2.7 %collective-permute-start.5 = (f32[18,6,256]{2,1,0:T(8,128)}, f32[18,6,256]{2,1,0:T(8,128)S(1)}, u32[]{:S(2)}, u32[]{:S(2)}) collective-permute-start(f32[18,6,256]{2,1,0:T(8,128)} %maximum_bitcast_fusion.1), channel_id=1, source_target_pairs={{1,0},{2,1},{3,2},{4,3},{5,4},{6,5},{7,6},{8,7},{9,8},{10,9},{11,1... | collective-permute-start | bytes 331784 | tf_op jit(solution)/shard_map/ppermute | solution.py:25
  9.4 7.6 %collective-permute-start.4 = (f32[18,6,256]{2,1,0:T(8,128)}, f32[18,6,256]{2,1,0:T(8,128)S(1)}, u32[]{:S(2)}, u32[]{:S(2)}) collective-permute-start(f32[18,6,256]{2,1,0:T(8,128)} %maximum_bitcast_fusion), channel_id=1, source_target_pairs={{0,1},{1,2},{2,3},{3,4},{4,5},{5,6},{6,7},{7,8},{8,9},{9,10},{10,1... | collective-permute-start | bytes 331784 | tf_op jit(solution)/shard_map/ppermute | solution.py:25
  17.0 1.0 slice_bitcast_fusion.1
  18.0 2.2 %collective-permute-start = (f32[6,256,128]{2,1,0:T(8,128)}, f32[6,256,128]{2,1,0:T(8,128)}, u32[]{:S(2)}, u32[]{:S(2)}) collective-permute-start(f32[6,256,128]{2,1,0:T(8,128)} %get-tuple-element.17), channel_id=1, source_target_pairs={{0,32},{32,64},{64,96},{1,33},{33,65},{65,97},{2,34},{34,66},{66,9... | collective-permute-start | bytes 2359304 | tf_op jit(solution)/shard_map/ppermute | solution.py:25
  24.1 0.8 constant_dynamic-slice_fusion.1
  25.0 1.0 copy.39
  26.1 0.8 copy-done.8
  27.7 0.9 slice-done
  28.8 0.8 copy-done.6
  30.4 1.5 %collective-permute-start.6 = (f32[288,256]{1,0:T(8,128)}, f32[288,256]{1,0:T(8,128)}, u32[]{:S(2)}, u32[]{:S(2)}) collective-permute-start(f32[288,256]{1,0:T(8,128)} %pad_maximum_fusion), channel_id=1, source_target_pairs={{0,32},{32,64},{64,96},{96,0},{1,33},{33,65},{65,97},{97,1},{2,34}... | collective-permute-start | bytes 884744 | tf_op jit(solution)/shard_map/ppermute | solution.py:222
  33.1 1.5 %collective-permute-start.8 = (f32[144,256]{1,0:T(8,128)S(1)}, f32[144,256]{1,0:T(8,128)S(1)}, u32[]{:S(2)}, u32[]{:S(2)}) collective-permute-start(f32[144,256]{1,0:T(8,128)S(1)} %broadcast_select_fusion), channel_id=1, source_target_pairs={{0,64},{32,96},{64,0},{96,32},{1,65},{33,97},{65,1},{97,33},{2,66}... | collective-permute-start | bytes 442376 | tf_op jit(solution)/shard_map/ppermute | solution.py:222
  34.5 1.0 slice_bitcast_fusion
  35.5 1.3 %collective-permute-start.1 = (s32[6,256,128]{2,1,0:T(8,128)}, s32[6,256,128]{2,1,0:T(8,128)S(1)}, u32[]{:S(2)}, u32[]{:S(2)}) collective-permute-start(s32[6,256,128]{2,1,0:T(8,128)} %get-tuple-element.15), channel_id=1, source_target_pairs={{0,32},{32,64},{64,96},{1,33},{33,65},{65,97},{2,34},{34,66},{66,9... | collective-permute-start | bytes 2359304 | tf_op jit(solution)/shard_map/ppermute | solution.py:25
  36.9 6.9 %collective-permute-done.8 = f32[144,256]{1,0:T(8,128)S(1)} collective-permute-done((f32[144,256]{1,0:T(8,128)S(1)}, f32[144,256]{1,0:T(8,128)S(1)}, u32[]{:S(2)}, u32[]{:S(2)}) %collective-permute-start.8) | collective-permute-done | bytes 147488 | tf_op jit(solution)/shard_map/ppermute | solution.py:222
  43.8 1.3 %collective-permute-start.2 = (f32[6,256,128]{2,1,0:T(8,128)S(1)}, f32[6,256,128]{2,1,0:T(8,128)}, u32[]{:S(2)}, u32[]{:S(2)}) collective-permute-start(f32[6,256,128]{2,1,0:T(8,128)S(1)} %get-tuple-element.16), channel_id=1, source_target_pairs={{32,0},{64,32},{96,64},{33,1},{65,33},{97,65},{34,2},{66,34},{98,6... | collective-permute-start | bytes 2359304 | tf_op jit(solution)/shard_map/ppermute | solution.py:25
  45.1 1.3 %collective-permute-start.3 = (s32[6,256,128]{2,1,0:T(8,128)S(1)}, s32[6,256,128]{2,1,0:T(8,128)}, u32[]{:S(2)}, u32[]{:S(2)}) collective-permute-start(s32[6,256,128]{2,1,0:T(8,128)S(1)} %get-tuple-element.14), channel_id=1, source_target_pairs={{32,0},{64,32},{96,64},{33,1},{65,33},{97,65},{34,2},{66,34},{98,6... | collective-permute-start | bytes 2359304 | tf_op jit(solution)/shard_map/ppermute | solution.py:25
  46.6 1.3 %fusion.4 = (f32[144,256]{1,0:T(8,128)S(1)}, f32[144,256]{1,0:T(8,128)S(1)}, f32[144,256]{1,0:T(8,128)S(1)}) fusion(f32[144,256]{1,0:T(8,128)S(1)} %concatenate.44, f32[144,256]{1,0:T(8,128)S(1)} %concatenate.45, f32[288,256]{1,0:T(8,128)} %collective-permute-done.7, f32[144,256]{1,0:T(8,128)} %copy-done.11, f32[288,256]{1,0:T(8,128)} %collective-permute-done.6, ...), kind=kLoop, calls=%fused_computation.14 | loop fusion | flops 258048 | bytes 1622017 | tf_op jit(solution)/shard_map/add | solution.py:229
  47.9 3.8 %collective-permute-start.10 = (f32[144,256]{1,0:T(8,128)S(1)}, f32[144,256]{1,0:T(8,128)S(1)}, u32[]{:S(2)}, u32[]{:S(2)}) collective-permute-start(f32[144,256]{1,0:T(8,128)S(1)} %get-tuple-element.18.d0_ref), channel_id=1, source_target_pairs={{0,64},{32,96},{64,0},{96,32},{1,65},{33,97},{65,1},{97,33},{2,66}... | collective-permute-start | bytes 442376 | tf_op jit(solution)/shard_map/ppermute | solution.py:235
  51.7 17.9 %collective-permute-done.10.d2_ref = f32[144,256]{1,0:T(8,128)S(1)} collective-permute-done((f32[144,256]{1,0:T(8,128)S(1)}, f32[144,256]{1,0:T(8,128)S(1)}, u32[]{:S(2)}, u32[]{:S(2)}) %collective-permute-start.10) | collective-permute-done | bytes 147488 | tf_op jit(solution)/shard_map/ppermute | solution.py:235
  73.2 3.9 %collective-permute-done.9.d1_ref = f32[144,256]{1,0:T(8,128)S(1)} collective-permute-done((f32[144,256]{1,0:T(8,128)S(1)}, f32[144,256]{1,0:T(8,128)S(1)}, u32[]{:S(2)}, u32[]{:S(2)}) %collective-permute-start.9) | collective-permute-done | bytes 147488 | tf_op jit(solution)/shard_map/ppermute | solution.py:235
  78.0 28.1 %shard_map.86 = f32[8,256,128]{2,1,0:T(8,128)} custom-call(s32[6]{0:T(128)} %pad_add_fusion.sc_ref, f32[8]{0:T(128)} %ctab_ref.1, f32[8]{0:T(128)} %htab_ref.1, f32[8,256,128]{2,1,0:T(8,128)} %bitcast.83, s32[8,256,128]{2,1,0:T(8,128)} %bitcast.85, f32[6,256,128]{2,1,0:T(8,128)} %collective-permute-done.tb_ref, s32[6,256,128]{2,1,0:T(8,128)} %copy-done.3, ...), custom_call_target="tpu_custom_call" | custom-call | tf_op jit(solution)/shard_map/pallas_call | solution.py:243
  (78 shorter events, 11.2 us)
Async XLA Ops:
  0.6 1.1 copy-start.15
  1.8 2.3 %copy-start.1 = (s32[8,1,256,128]{3,2,1,0:T(8,128)S(1)}, s32[8,1,256,128]{3,2,1,0:T(8,128)}, u32[]{:S(2)}) copy-start(s32[8,1,256,128]{3,2,1,0:T(8,128)} %param.8) | copy-start | bytes 3145732
  4.1 12.9 %copy-start = (f32[8,1,256,128]{3,2,1,0:T(8,128)S(1)}, f32[8,1,256,128]{3,2,1,0:T(8,128)}, u32[]{:S(2)}) copy-start(f32[8,1,256,128]{3,2,1,0:T(8,128)} %param.7) | copy-start | bytes 3145732
  6.0 21.7 %collective-permute-start.5 = (f32[18,6,256]{2,1,0:T(8,128)}, f32[18,6,256]{2,1,0:T(8,128)S(1)}, u32[]{:S(2)}, u32[]{:S(2)}) collective-permute-start(f32[18,6,256]{2,1,0:T(8,128)} %maximum_bitcast_fusion.1), channel_id=1, source_target_pairs={{1,0},{2,1},{3,2},{4,3},{5,4},{6,5},{7,6},{8,7},{9,8},{10,9},{11,1... | collective-permute-start | bytes 331784 | tf_op jit(solution)/shard_map/ppermute | solution.py:25
  9.4 17.7 %collective-permute-start.4 = (f32[18,6,256]{2,1,0:T(8,128)}, f32[18,6,256]{2,1,0:T(8,128)S(1)}, u32[]{:S(2)}, u32[]{:S(2)}) collective-permute-start(f32[18,6,256]{2,1,0:T(8,128)} %maximum_bitcast_fusion), channel_id=1, source_target_pairs={{0,1},{1,2},{2,3},{3,4},{4,5},{5,6},{6,7},{7,8},{8,9},{9,10},{10,1... | collective-permute-start | bytes 331784 | tf_op jit(solution)/shard_map/ppermute | solution.py:25
  18.0 59.1 %collective-permute-start = (f32[6,256,128]{2,1,0:T(8,128)}, f32[6,256,128]{2,1,0:T(8,128)}, u32[]{:S(2)}, u32[]{:S(2)}) collective-permute-start(f32[6,256,128]{2,1,0:T(8,128)} %get-tuple-element.17), channel_id=1, source_target_pairs={{0,32},{32,64},{64,96},{1,33},{33,65},{65,97},{2,34},{34,66},{66,9... | collective-permute-start | bytes 2359304 | tf_op jit(solution)/shard_map/ppermute | solution.py:25
  24.9 1.0 copy-start.9
  27.7 1.1 copy-start.4
  27.7 1.0 slice-start
  28.7 0.9 copy-start.6
  30.4 14.6 %collective-permute-start.6 = (f32[288,256]{1,0:T(8,128)}, f32[288,256]{1,0:T(8,128)}, u32[]{:S(2)}, u32[]{:S(2)}) collective-permute-start(f32[288,256]{1,0:T(8,128)} %pad_maximum_fusion), channel_id=1, source_target_pairs={{0,32},{32,64},{64,96},{96,0},{1,33},{33,65},{65,97},{97,1},{2,34}... | collective-permute-start | bytes 884744 | tf_op jit(solution)/shard_map/ppermute | solution.py:222
  32.7 13.9 %collective-permute-start.7 = (f32[288,256]{1,0:T(8,128)}, f32[288,256]{1,0:T(8,128)}, u32[]{:S(2)}, u32[]{:S(2)}) collective-permute-start(f32[288,256]{1,0:T(8,128)} %pad_maximum_fusion.1), channel_id=1, source_target_pairs={{0,96},{32,0},{64,32},{96,64},{1,97},{33,1},{65,33},{97,65},{2,98}... | collective-permute-start | bytes 884744 | tf_op jit(solution)/shard_map/ppermute | solution.py:222
  33.1 10.7 %collective-permute-start.8 = (f32[144,256]{1,0:T(8,128)S(1)}, f32[144,256]{1,0:T(8,128)S(1)}, u32[]{:S(2)}, u32[]{:S(2)}) collective-permute-start(f32[144,256]{1,0:T(8,128)S(1)} %broadcast_select_fusion), channel_id=1, source_target_pairs={{0,64},{32,96},{64,0},{96,32},{1,65},{33,97},{65,1},{97,33},{2,66}... | collective-permute-start | bytes 442376 | tf_op jit(solution)/shard_map/ppermute | solution.py:222
  34.5 11.9 %copy-start.7 = (f32[1,1,256,128]{3,2,1,0:T(8,128)S(1)}, f32[1,1,256,128]{3,2,1,0:T(8,128)}, u32[]{:S(2)}) copy-start(f32[1,1,256,128]{3,2,1,0:T(8,128)} %get-tuple-element.6) | copy-start | bytes 393220
  35.5 41.6 %collective-permute-start.1 = (s32[6,256,128]{2,1,0:T(8,128)}, s32[6,256,128]{2,1,0:T(8,128)S(1)}, u32[]{:S(2)}, u32[]{:S(2)}) collective-permute-start(s32[6,256,128]{2,1,0:T(8,128)} %get-tuple-element.15), channel_id=1, source_target_pairs={{0,32},{32,64},{64,96},{1,33},{33,65},{65,97},{2,34},{34,66},{66,9... | collective-permute-start | bytes 2359304 | tf_op jit(solution)/shard_map/ppermute | solution.py:25
  43.8 2.7 %copy-start.11 = (f32[144,256]{1,0:T(8,128)}, f32[144,256]{1,0:T(8,128)S(1)}, u32[]{:S(2)}) copy-start(f32[144,256]{1,0:T(8,128)S(1)} %collective-permute-done.8) | copy-start | bytes 442372
  43.8 33.4 %collective-permute-start.2 = (f32[6,256,128]{2,1,0:T(8,128)S(1)}, f32[6,256,128]{2,1,0:T(8,128)}, u32[]{:S(2)}, u32[]{:S(2)}) collective-permute-start(f32[6,256,128]{2,1,0:T(8,128)S(1)} %get-tuple-element.16), channel_id=1, source_target_pairs={{32,0},{64,32},{96,64},{33,1},{65,33},{97,65},{34,2},{66,34},{98,6... | collective-permute-start | bytes 2359304 | tf_op jit(solution)/shard_map/ppermute | solution.py:25
  45.1 32.1 %collective-permute-start.3 = (s32[6,256,128]{2,1,0:T(8,128)S(1)}, s32[6,256,128]{2,1,0:T(8,128)}, u32[]{:S(2)}, u32[]{:S(2)}) collective-permute-start(s32[6,256,128]{2,1,0:T(8,128)S(1)} %get-tuple-element.14), channel_id=1, source_target_pairs={{32,0},{64,32},{96,64},{33,1},{65,33},{97,65},{34,2},{66,34},{98,6... | collective-permute-start | bytes 2359304 | tf_op jit(solution)/shard_map/ppermute | solution.py:25
  47.9 24.5 %copy-start.2 = (f32[144,256]{1,0:T(8,128)}, f32[144,256]{1,0:T(8,128)S(1)}, u32[]{:S(2)}) copy-start(f32[144,256]{1,0:T(8,128)S(1)} %get-tuple-element.18.d0_ref) | copy-start | bytes 442372
  47.9 21.8 %collective-permute-start.10 = (f32[144,256]{1,0:T(8,128)S(1)}, f32[144,256]{1,0:T(8,128)S(1)}, u32[]{:S(2)}, u32[]{:S(2)}) collective-permute-start(f32[144,256]{1,0:T(8,128)S(1)} %get-tuple-element.18.d0_ref), channel_id=1, source_target_pairs={{0,64},{32,96},{64,0},{96,32},{1,65},{33,97},{65,1},{97,33},{2,66}... | collective-permute-start | bytes 442376 | tf_op jit(solution)/shard_map/ppermute | solution.py:235
  69.7 1.3 %copy-start.12 = (f32[144,256]{1,0:T(8,128)}, f32[144,256]{1,0:T(8,128)S(1)}, u32[]{:S(2)}) copy-start(f32[144,256]{1,0:T(8,128)S(1)} %collective-permute-done.10.d2_ref) | copy-start | bytes 442372
  69.7 2.7 %collective-permute-start.11 = (f32[144,256]{1,0:T(8,128)S(1)}, f32[144,256]{1,0:T(8,128)S(1)}, u32[]{:S(2)}, u32[]{:S(2)}) collective-permute-start(f32[144,256]{1,0:T(8,128)S(1)} %get-tuple-element.18.d0_ref), channel_id=1, source_target_pairs={{0,96},{32,0},{64,32},{96,64},{1,97},{33,1},{65,33},{97,65},{2,98}... | collective-permute-start | bytes 442376 | tf_op jit(solution)/shard_map/ppermute | solution.py:235
  72.4 4.7 %collective-permute-start.9 = (f32[144,256]{1,0:T(8,128)S(1)}, f32[144,256]{1,0:T(8,128)S(1)}, u32[]{:S(2)}, u32[]{:S(2)}) collective-permute-start(f32[144,256]{1,0:T(8,128)S(1)} %get-tuple-element.18.d0_ref), channel_id=1, source_target_pairs={{0,32},{32,64},{64,96},{96,0},{1,33},{33,65},{65,97},{97,1},{2,34}... | collective-permute-start | bytes 442376 | tf_op jit(solution)/shard_map/ppermute | solution.py:235
  77.1 0.9 copy-start.3
  (6 other events, 4.5 us)
where the time goes:
time: 107 us; the launch traced here: 106 us
  waiting for transfers between devices  29.5 us (28%)
  Pallas kernels  28.1 us (26%)
  starting transfers between devices  23.4 us (22%)
  local copies, waits for them, and re-layouts  16.7 us (16%)
  other arithmetic  4.79 us (4%)
  between operations  3.62 us (3%)
    pallas_call x1, Pallas kernels, local_body(): pl.pallas_call(kern, out_shape=jax.ShapeDtypeStruct((local_depth, nx, str...  28.1 us
    ppermute x3, waiting for transfers between devices, local_body(): slots.append(lax.ppermute(power_w, 'depth', route))  22.6 us
    ppermute x6, starting transfers between devices, from_behind(): return lax.ppermute(block, axis, route)  16.4 us
    unnamed x39, local copies, waits for them, and re-layouts  8.58 us
    ppermute x3, waiting for transfers between devices, local_body(): got = lax.ppermute(sent, 'depth', route)  6.89 us
    ppermute x3, starting transfers between devices, local_body(): slots.append(lax.ppermute(power_w, 'depth', route))  3.83 us
    ppermute x3, starting transfers between devices, local_body(): got = lax.ppermute(sent, 'depth', route)  3.2 us
  transfers between devices with their start and end apart: 12, of which 4 were waited for; matrix products, arithmetic and copies ran while one was open for 11% of the time, Pallas kernels for 0%

commit v1 on v0

--- a/solution.py
+++ b/solution.py
@@ -141,7 +141,7 @@
         inv_s[l] = 1.0 / diag
         return c
 
-    lax.fori_loop(0, ze, faces, 0)
+    lax.fori_loop(1, ze - 1, faces, 0)
 
     def relax(src, l):
         t = t_s[src, l]
@@ -202,7 +202,8 @@
 
     side = jnp.concatenate([ylo[:2 * local_depth].reshape(2, local_depth, HALO, nx),
                             yhi[:2 * local_depth].reshape(2, local_depth, HALO, nx)], axis=2)
-    corner_of = {1: side[:, local_depth - HALO:], dies - 1: side[:, :HALO]}
+    cb = from_behind(side[:, local_depth - HALO:], "depth", 1)
+    ca = from_behind(side[:, :HALO], "depth", -1)
 
     def pick(die):
         at = die_layer[die] - first_layer
@@ -213,17 +214,9 @@
         return jnp.where((at >= 0) & (at < local_depth), layer, 0.0)
 
     die_temp = pick(g)
-    got_corners = {}
     for o in range(1, dies):
         route = [(i, (i + o) % depth_n) for i in range(depth_n)]
-        sent = pick((g + o) % dies)
-        if o in corner_of:
-            sent = jnp.concatenate([sent, corner_of[o].reshape(-1, nx)])
-        got = lax.ppermute(sent, "depth", route)
-        die_temp = die_temp + got[:ye]
-        if o in corner_of:
-            got_corners[o] = got[ye:].reshape(2, HALO, 2 * HALO, nx)
-    cb, ca = got_corners[1], got_corners[dies - 1]
+        die_temp = die_temp + lax.ppermute(pick((g + o) % dies), "depth", route)
     dyn_w = widen(dyn_power[0, 0].T, ylo[nf - 2], yhi[nf - 2])
     leak_w = widen(leak_ref[0, 0].T, ylo[nf - 1], yhi[nf - 1])
     power_w = dyn_w + leak_w * jnp.exp(LEAK_SLOPE * die_temp)

time: 107 us -> 106 us (level)
  the two profiles are of different devices: /device:TPU:70 before, /device:TPU:25 now
where the time goes in v1:
time: 106 us
  starting transfers between devices  30.1 us (28%)
  Pallas kernels  27.6 us (26%)
  local copies, waits for them, and re-layouts  19.6 us (18%)
  waiting for transfers between devices  19.6 us (18%)
  other arithmetic  5.35 us (5%)
  between operations  3.67 us (3%)
    pallas_call x1, Pallas kernels, local_body(): pl.pallas_call(kern, out_shape=jax.ShapeDtypeStruct((local_depth, nx, str...  27.6 us
    ppermute x8, starting transfers between devices, from_behind(): return lax.ppermute(block, axis, route)  25.1 us
    ppermute x8, waiting for transfers between devices, from_behind(): return lax.ppermute(block, axis, route)  10.7 us
    ppermute x3, waiting for transfers between devices, local_body(): slots.append(lax.ppermute(power_w, 'depth', route))  8.94 us
    unnamed x59, local copies, waits for them, and re-layouts  8.69 us
    concatenate x6, local copies, waits for them, and re-layouts, widen(): jnp.concatenate([jnp.zeros((PAD_Y - HALO, nx), jnp.float32), lo, centre,...  5.76 us
    ppermute x3, starting transfers between devices, local_body(): die_temp = die_temp + lax.ppermute(pick((g + o) % dies), 'depth', route)  3.3 us
  transfers between devices with their start and end apart: 14, of which 4 were waited for; matrix products, arithmetic and copies ran while one was open for 15% of the time, Pallas kernels for 0%

profile of v1, /device:TPU:25, one launch (start us, length us, event | category | flops | bytes accessed | tf_op | source)
XLA Modules:
  0.0 105.8 jit_solution(4406233633021046637)
XLA Ops:
  0.6 1.0 copy.15
  1.8 1.6 %copy.10 = s32[8,1,256,128]{2,3,0,1:T(8,128)S(1)} copy(s32[8,1,256,128]{3,2,1,0:T(8,128)} %param.8) | data formatting | bytes 2097152 | tf_op args[1]
  4.6 7.9 %collective-permute-start.5 = (f32[18,6,256]{2,1,0:T(8,128)}, f32[18,6,256]{2,1,0:T(8,128)S(1)}, u32[]{:S(2)}, u32[]{:S(2)}) collective-permute-start(f32[18,6,256]{2,1,0:T(8,128)} %maximum_bitcast_fusion.1), channel_id=1, source_target_pairs={{1,0},{2,1},{3,2},{4,3},{5,4},{6,5},{7,6},{8,7},{9,8},{10,9},{11,1... | collective-permute-start | bytes 331784 | tf_op jit(solution)/shard_map/ppermute | solution.py:25
  13.1 1.9 %collective-permute-start.4 = (f32[18,6,256]{2,1,0:T(8,128)}, f32[18,6,256]{2,1,0:T(8,128)S(1)}, u32[]{:S(2)}, u32[]{:S(2)}) collective-permute-start(f32[18,6,256]{2,1,0:T(8,128)} %maximum_bitcast_fusion), channel_id=1, source_target_pairs={{0,1},{1,2},{2,3},{3,4},{4,5},{5,6},{6,7},{7,8},{8,9},{9,10},{10,1... | collective-permute-start | bytes 331784 | tf_op jit(solution)/shard_map/ppermute | solution.py:25
  15.2 3.5 %collective-permute-start = (f32[6,256,128]{2,1,0:T(8,128)S(1)}, f32[6,256,128]{2,1,0:T(8,128)}, u32[]{:S(2)}, u32[]{:S(2)}) collective-permute-start(f32[6,256,128]{2,1,0:T(8,128)S(1)} %get-tuple-element.15), channel_id=1, source_target_pairs={{0,32},{32,64},{64,96},{1,33},{33,65},{65,97},{2,34},{34,66},{66,9... | collective-permute-start | bytes 2359304 | tf_op jit(solution)/shard_map/ppermute | solution.py:25
  25.6 2.4 %collective-permute-start.8 = (f32[144,256]{1,0:T(8,128)}, f32[144,256]{1,0:T(8,128)}, u32[]{:S(2)}, u32[]{:S(2)}) collective-permute-start(f32[144,256]{1,0:T(8,128)} %broadcast_select_fusion.2), channel_id=1, source_target_pairs={{0,32},{32,64},{64,96},{96,0},{1,33},{33,65},{65,97},{97,1},{2,34}... | collective-permute-start | bytes 442376 | tf_op jit(solution)/shard_map/ppermute | solution.py:219
  29.7 0.9 slice-done
  31.4 3.6 %collective-permute-start.6 = (f32[2,6,12,256]{3,2,1,0:T(8,128)}, f32[2,6,12,256]{3,2,1,0:T(8,128)}, u32[]{:S(2)}, u32[]{:S(2)}) collective-permute-start(f32[2,6,12,256]{3,2,1,0:T(8,128)} %get-tuple-element.17), channel_id=1, source_target_pairs={{0,32},{32,64},{64,96},{1,33},{33,65},{65,97},{2,34},{34,66},{66,9... | collective-permute-start | bytes 442376 | tf_op jit(solution)/shard_map/ppermute | solution.py:25
  35.0 1.0 slice_bitcast_fusion
  36.1 1.9 %collective-permute-start.1 = (s32[6,256,128]{2,1,0:T(8,128)}, s32[6,256,128]{2,1,0:T(8,128)S(1)}, u32[]{:S(2)}, u32[]{:S(2)}) collective-permute-start(s32[6,256,128]{2,1,0:T(8,128)} %get-tuple-element.13), channel_id=1, source_target_pairs={{0,32},{32,64},{64,96},{1,33},{33,65},{65,97},{2,34},{34,66},{66,9... | collective-permute-start | bytes 2359304 | tf_op jit(solution)/shard_map/ppermute | solution.py:25
  38.0 2.5 %collective-permute-start.2 = (f32[6,256,128]{2,1,0:T(8,128)S(1)}, f32[6,256,128]{2,1,0:T(8,128)}, u32[]{:S(2)}, u32[]{:S(2)}) collective-permute-start(f32[6,256,128]{2,1,0:T(8,128)S(1)} %get-tuple-element.14), channel_id=1, source_target_pairs={{32,0},{64,32},{96,64},{33,1},{65,33},{97,65},{34,2},{66,34},{98,6... | collective-permute-start | bytes 2359304 | tf_op jit(solution)/shard_map/ppermute | solution.py:25
  41.1 1.9 %collective-permute-start.3 = (s32[6,256,128]{2,1,0:T(8,128)S(1)}, s32[6,256,128]{2,1,0:T(8,128)}, u32[]{:S(2)}, u32[]{:S(2)}) collective-permute-start(s32[6,256,128]{2,1,0:T(8,128)S(1)} %get-tuple-element.12), channel_id=1, source_target_pairs={{32,0},{64,32},{96,64},{33,1},{65,33},{97,65},{34,2},{66,34},{98,6... | collective-permute-start | bytes 2359304 | tf_op jit(solution)/shard_map/ppermute | solution.py:25
  43.9 1.9 %concatenate.36 = f32[144,256]{1,0:T(8,128)} concatenate(f32[2,256]{1,0:T(2,128)S(1)} %copy-done.13, f32[6,256]{1,0:T(8,128)S(1)} %copy-done.24, f32[128,256]{1,0:T(8,128)S(1)} %bitcast.97, f32[6,256]{1,0:T(8,128)S(1)} %copy-done.21, f32[2,256]{1,0:T(2,128)S(1)} %copy-done.13), dimensions={0} | concatenate | bytes 294912 | tf_op jit(solution)/shard_map/concatenate | solution.py:200
  45.8 1.9 %concatenate.35 = f32[144,256]{1,0:T(8,128)} concatenate(f32[2,256]{1,0:T(2,128)S(1)} %copy-done.13, f32[6,256]{1,0:T(8,128)S(1)} %copy-done.23, f32[128,256]{1,0:T(8,128)S(1)} %bitcast.92, f32[6,256]{1,0:T(8,128)S(1)} %copy-done.20, f32[2,256]{1,0:T(2,128)S(1)} %copy-done.13), dimensions={0} | concatenate | bytes 294912 | tf_op jit(solution)/shard_map/concatenate | solution.py:200
  47.7 1.9 %concatenate.34 = f32[144,256]{1,0:T(8,128)} concatenate(f32[2,256]{1,0:T(2,128)S(1)} %copy-done.13, f32[6,256]{1,0:T(8,128)S(1)} %copy-done.22, f32[128,256]{1,0:T(8,128)S(1)} %bitcast.91, f32[6,256]{1,0:T(8,128)S(1)} %copy-done.19, f32[2,256]{1,0:T(2,128)S(1)} %copy-done.13), dimensions={0} | concatenate | bytes 294912 | tf_op jit(solution)/shard_map/concatenate | solution.py:200
  49.6 1.9 %collective-permute-start.7 = (f32[2,6,12,256]{3,2,1,0:T(8,128)}, f32[2,6,12,256]{3,2,1,0:T(8,128)S(1)}, u32[]{:S(2)}, u32[]{:S(2)}) collective-permute-start(f32[2,6,12,256]{3,2,1,0:T(8,128)} %get-tuple-element.16), channel_id=1, source_target_pairs={{32,0},{64,32},{96,64},{33,1},{65,33},{97,65},{34,2},{66,34},{98,6... | collective-permute-start | bytes 442376 | tf_op jit(solution)/shard_map/ppermute | solution.py:25
  51.5 1.3 %multiply_add_fusion.d0_ref = f32[144,256]{1,0:T(8,128)S(1)} fusion(f32[144,256]{1,0:T(8,128)} %concatenate.34, f32[144,256]{1,0:T(8,128)} %concatenate.35, f32[144,256]{1,0:T(8,128)} %copy-done.15, f32[144,256]{1,0:T(8,128)} %collective-permute-done.9, f32[144,256]{1,0:T(8,128)} %collective-permute-done.8, f32[144,256]{1,0:T(8,128)S(1)} %copy-done.10, ...), kind=kLoop, calls=%fused_computation.10 | loop fusion | flops 258048 | bytes 1032193 | tf_op jit(solution)/shard_map/add | solution.py:222
  52.8 10.7 %collective-permute-done.7.ca_ref = f32[2,6,12,256]{3,2,1,0:T(8,128)S(1)} collective-permute-done((f32[2,6,12,256]{3,2,1,0:T(8,128)}, f32[2,6,12,256]{3,2,1,0:T(8,128)S(1)}, u32[]{:S(2)}, u32[]{:S(2)}) %collective-permute-start.7) | collective-permute-done | bytes 147488 | tf_op jit(solution)/shard_map/ppermute | solution.py:25
  63.4 2.1 %collective-permute-done.11.d1_ref = f32[144,256]{1,0:T(8,128)S(1)} collective-permute-done((f32[144,256]{1,0:T(8,128)S(1)}, f32[144,256]{1,0:T(8,128)S(1)}, u32[]{:S(2)}, u32[]{:S(2)}) %collective-permute-start.11) | collective-permute-done | bytes 147488 | tf_op jit(solution)/shard_map/ppermute | solution.py:228
  67.4 3.3 %collective-permute-done.12.d2_ref = f32[144,256]{1,0:T(8,128)S(1)} collective-permute-done((f32[144,256]{1,0:T(8,128)S(1)}, f32[144,256]{1,0:T(8,128)S(1)}, u32[]{:S(2)}, u32[]{:S(2)}) %collective-permute-start.12) | collective-permute-done | bytes 147488 | tf_op jit(solution)/shard_map/ppermute | solution.py:228
  71.4 1.7 %collective-permute-start.13 = (f32[144,256]{1,0:T(8,128)S(1)}, f32[144,256]{1,0:T(8,128)}, u32[]{:S(2)}, u32[]{:S(2)}) collective-permute-start(f32[144,256]{1,0:T(8,128)S(1)} %multiply_add_fusion.d0_ref), channel_id=1, source_target_pairs={{0,96},{32,0},{64,32},{96,64},{1,97},{33,1},{65,33},{97,65},{2,98}... | collective-permute-start | bytes 442376 | tf_op jit(solution)/shard_map/ppermute | solution.py:228
  73.9 3.5 %collective-permute-done.13.d3_ref = f32[144,256]{1,0:T(8,128)} collective-permute-done((f32[144,256]{1,0:T(8,128)S(1)}, f32[144,256]{1,0:T(8,128)}, u32[]{:S(2)}, u32[]{:S(2)}) %collective-permute-start.13) | collective-permute-done | bytes 147488 | tf_op jit(solution)/shard_map/ppermute | solution.py:228
  77.4 0.8 copy-done.3
  78.3 27.6 %shard_map.86 = f32[8,256,128]{2,1,0:T(8,128)} custom-call(s32[6]{0:T(128)} %pad_add_fusion.sc_ref, f32[8]{0:T(128)} %ctab_ref.1, f32[8]{0:T(128)} %htab_ref.1, f32[8,256,128]{2,1,0:T(8,128)} %bitcast.83, s32[8,256,128]{2,1,0:T(8,128)} %bitcast.85, f32[6,256,128]{2,1,0:T(8,128)} %collective-permute-done.tb_ref, s32[6,256,128]{2,1,0:T(8,128)} %copy-done.3, ...), custom_call_target="tpu_custom_call" | custom-call | tf_op jit(solution)/shard_map/pallas_call | solution.py:236
  (96 shorter events, 13.5 us)
Async XLA Ops:
  1.7 2.2 %copy-start.6 = (f32[1,1,256,128]{2,3,1,0:T(8,128)}, f32[1,1,256,128]{2,3,1,0:T(8,128)S(1)}, u32[]{:S(2)}) copy-start(f32[1,1,256,128]{2,3,1,0:T(8,128)S(1)} %copy.15) | copy-start | bytes 393220
  1.8 2.1 %copy-start.8 = (f32[1,1,256,128]{2,3,1,0:T(8,128)}, f32[1,1,256,128]{2,3,1,0:T(8,128)S(1)}, u32[]{:S(2)}) copy-start(f32[1,1,256,128]{2,3,1,0:T(8,128)S(1)} %copy.16) | copy-start | bytes 393220
  4.6 19.0 %collective-permute-start.5 = (f32[18,6,256]{2,1,0:T(8,128)}, f32[18,6,256]{2,1,0:T(8,128)S(1)}, u32[]{:S(2)}, u32[]{:S(2)}) collective-permute-start(f32[18,6,256]{2,1,0:T(8,128)} %maximum_bitcast_fusion.1), channel_id=1, source_target_pairs={{1,0},{2,1},{3,2},{4,3},{5,4},{6,5},{7,6},{8,7},{9,8},{10,9},{11,1... | collective-permute-start | bytes 331784 | tf_op jit(solution)/shard_map/ppermute | solution.py:25
  13.1 11.1 %collective-permute-start.4 = (f32[18,6,256]{2,1,0:T(8,128)}, f32[18,6,256]{2,1,0:T(8,128)S(1)}, u32[]{:S(2)}, u32[]{:S(2)}) collective-permute-start(f32[18,6,256]{2,1,0:T(8,128)} %maximum_bitcast_fusion), channel_id=1, source_target_pairs={{0,1},{1,2},{2,3},{3,4},{4,5},{5,6},{6,7},{7,8},{8,9},{9,10},{10,1... | collective-permute-start | bytes 331784 | tf_op jit(solution)/shard_map/ppermute | solution.py:25
  15.2 62.2 %collective-permute-start = (f32[6,256,128]{2,1,0:T(8,128)S(1)}, f32[6,256,128]{2,1,0:T(8,128)}, u32[]{:S(2)}, u32[]{:S(2)}) collective-permute-start(f32[6,256,128]{2,1,0:T(8,128)S(1)} %get-tuple-element.15), channel_id=1, source_target_pairs={{0,32},{32,64},{64,96},{1,33},{33,65},{65,97},{2,34},{34,66},{66,9... | collective-permute-start | bytes 2359304 | tf_op jit(solution)/shard_map/ppermute | solution.py:25
  23.6 6.1 %copy-start.4 = (f32[18,6,256]{2,1,0:T(8,128)}, f32[18,6,256]{2,1,0:T(8,128)S(1)}, u32[]{:S(2)}) copy-start(f32[18,6,256]{2,1,0:T(8,128)S(1)} %collective-permute-done.5.yhi_ref) | copy-start | bytes 331780
  24.2 5.5 %copy-start.5 = (f32[18,6,256]{2,1,0:T(8,128)}, f32[18,6,256]{2,1,0:T(8,128)S(1)}, u32[]{:S(2)}) copy-start(f32[18,6,256]{2,1,0:T(8,128)S(1)} %collective-permute-done.4.ylo_ref) | copy-start | bytes 331780
  24.9 4.6 %copy-start.12 = (f32[2,256]{1,0:T(2,128)}, f32[2,256]{1,0:T(2,128)S(1)}, u32[]{:S(2)}) copy-start(f32[2,256]{1,0:T(2,128)S(1)} %broadcast.6) | copy-start | bytes 6148
  25.6 10.5 %collective-permute-start.8 = (f32[144,256]{1,0:T(8,128)}, f32[144,256]{1,0:T(8,128)}, u32[]{:S(2)}, u32[]{:S(2)}) collective-permute-start(f32[144,256]{1,0:T(8,128)} %broadcast_select_fusion.2), channel_id=1, source_target_pairs={{0,32},{32,64},{64,96},{96,0},{1,33},{33,65},{65,97},{97,1},{2,34}... | collective-permute-start | bytes 442376 | tf_op jit(solution)/shard_map/ppermute | solution.py:219
  28.0 7.0 %copy-start.1 = (s32[8,1,256,128]{3,2,1,0:T(8,128)S(1)}, s32[8,1,256,128]{3,2,1,0:T(8,128)}, u32[]{:S(2)}) copy-start(s32[8,1,256,128]{3,2,1,0:T(8,128)} %param.8) | copy-start | bytes 3145732
  28.7 9.3 %collective-permute-start.9 = (f32[144,256]{1,0:T(8,128)}, f32[144,256]{1,0:T(8,128)}, u32[]{:S(2)}, u32[]{:S(2)}) collective-permute-start(f32[144,256]{1,0:T(8,128)} %broadcast_select_fusion.1), channel_id=1, source_target_pairs={{0,64},{32,96},{64,0},{96,32},{1,65},{33,97},{65,1},{97,33},{2,66}... | collective-permute-start | bytes 442376 | tf_op jit(solution)/shard_map/ppermute | solution.py:219
  29.6 10.9 %collective-permute-start.10 = (f32[144,256]{1,0:T(8,128)S(1)}, f32[144,256]{1,0:T(8,128)S(1)}, u32[]{:S(2)}, u32[]{:S(2)}) collective-permute-start(f32[144,256]{1,0:T(8,128)S(1)} %broadcast_select_fusion), channel_id=1, source_target_pairs={{0,96},{32,0},{64,32},{96,64},{1,97},{33,1},{65,33},{97,65},{2,98}... | collective-permute-start | bytes 442376 | tf_op jit(solution)/shard_map/ppermute | solution.py:219
  31.4 18.2 %collective-permute-start.6 = (f32[2,6,12,256]{3,2,1,0:T(8,128)}, f32[2,6,12,256]{3,2,1,0:T(8,128)}, u32[]{:S(2)}, u32[]{:S(2)}) collective-permute-start(f32[2,6,12,256]{3,2,1,0:T(8,128)} %get-tuple-element.17), channel_id=1, source_target_pairs={{0,32},{32,64},{64,96},{1,33},{33,65},{65,97},{2,34},{34,66},{66,9... | collective-permute-start | bytes 442376 | tf_op jit(solution)/shard_map/ppermute | solution.py:25
  35.0 8.0 %copy-start.11 = (f32[1,1,256,128]{3,2,1,0:T(8,128)S(1)}, f32[1,1,256,128]{3,2,1,0:T(8,128)}, u32[]{:S(2)}) copy-start(f32[1,1,256,128]{3,2,1,0:T(8,128)} %get-tuple-element.4) | copy-start | bytes 393220
  36.1 41.3 %collective-permute-start.1 = (s32[6,256,128]{2,1,0:T(8,128)}, s32[6,256,128]{2,1,0:T(8,128)S(1)}, u32[]{:S(2)}, u32[]{:S(2)}) collective-permute-start(s32[6,256,128]{2,1,0:T(8,128)} %get-tuple-element.13), channel_id=1, source_target_pairs={{0,32},{32,64},{64,96},{1,33},{33,65},{65,97},{2,34},{34,66},{66,9... | collective-permute-start | bytes 2359304 | tf_op jit(solution)/shard_map/ppermute | solution.py:25
  38.0 39.4 %collective-permute-start.2 = (f32[6,256,128]{2,1,0:T(8,128)S(1)}, f32[6,256,128]{2,1,0:T(8,128)}, u32[]{:S(2)}, u32[]{:S(2)}) collective-permute-start(f32[6,256,128]{2,1,0:T(8,128)S(1)} %get-tuple-element.14), channel_id=1, source_target_pairs={{32,0},{64,32},{96,64},{33,1},{65,33},{97,65},{34,2},{66,34},{98,6... | collective-permute-start | bytes 2359304 | tf_op jit(solution)/shard_map/ppermute | solution.py:25
  41.1 36.3 %collective-permute-start.3 = (s32[6,256,128]{2,1,0:T(8,128)S(1)}, s32[6,256,128]{2,1,0:T(8,128)}, u32[]{:S(2)}, u32[]{:S(2)}) collective-permute-start(s32[6,256,128]{2,1,0:T(8,128)S(1)} %get-tuple-element.12), channel_id=1, source_target_pairs={{32,0},{64,32},{96,64},{33,1},{65,33},{97,65},{34,2},{66,34},{98,6... | collective-permute-start | bytes 2359304 | tf_op jit(solution)/shard_map/ppermute | solution.py:25
  47.7 3.8 %copy-start.10 = (f32[144,256]{1,0:T(8,128)S(1)}, f32[144,256]{1,0:T(8,128)}, u32[]{:S(2)}) copy-start(f32[144,256]{1,0:T(8,128)} %concatenate.36) | copy-start | bytes 442372
  49.6 13.9 %collective-permute-start.7 = (f32[2,6,12,256]{3,2,1,0:T(8,128)}, f32[2,6,12,256]{3,2,1,0:T(8,128)S(1)}, u32[]{:S(2)}, u32[]{:S(2)}) collective-permute-start(f32[2,6,12,256]{3,2,1,0:T(8,128)} %get-tuple-element.16), channel_id=1, source_target_pairs={{32,0},{64,32},{96,64},{33,1},{65,33},{97,65},{34,2},{66,34},{98,6... | collective-permute-start | bytes 442376 | tf_op jit(solution)/shard_map/ppermute | solution.py:25
  52.8 21.1 %copy-start.2 = (f32[144,256]{1,0:T(8,128)}, f32[144,256]{1,0:T(8,128)S(1)}, u32[]{:S(2)}) copy-start(f32[144,256]{1,0:T(8,128)S(1)} %multiply_add_fusion.d0_ref) | copy-start | bytes 442372
  63.4 2.1 %copy-start.14 = (f32[2,6,12,256]{3,2,1,0:T(8,128)}, f32[2,6,12,256]{3,2,1,0:T(8,128)S(1)}, u32[]{:S(2)}) copy-start(f32[2,6,12,256]{3,2,1,0:T(8,128)S(1)} %collective-permute-done.7.ca_ref) | copy-start | bytes 442372
  63.4 2.1 %collective-permute-start.11 = (f32[144,256]{1,0:T(8,128)S(1)}, f32[144,256]{1,0:T(8,128)S(1)}, u32[]{:S(2)}, u32[]{:S(2)}) collective-permute-start(f32[144,256]{1,0:T(8,128)S(1)} %multiply_add_fusion.d0_ref), channel_id=1, source_target_pairs={{0,32},{32,64},{64,96},{96,0},{1,33},{33,65},{65,97},{97,1},{2,34}... | collective-permute-start | bytes 442376 | tf_op jit(solution)/shard_map/ppermute | solution.py:228
  66.2 4.6 %collective-permute-start.12 = (f32[144,256]{1,0:T(8,128)S(1)}, f32[144,256]{1,0:T(8,128)S(1)}, u32[]{:S(2)}, u32[]{:S(2)}) collective-permute-start(f32[144,256]{1,0:T(8,128)S(1)} %multiply_add_fusion.d0_ref), channel_id=1, source_target_pairs={{0,64},{32,96},{64,0},{96,32},{1,65},{33,97},{65,1},{97,33},{2,66}... | collective-permute-start | bytes 442376 | tf_op jit(solution)/shard_map/ppermute | solution.py:228
  71.4 6.0 %collective-permute-start.13 = (f32[144,256]{1,0:T(8,128)S(1)}, f32[144,256]{1,0:T(8,128)}, u32[]{:S(2)}, u32[]{:S(2)}) collective-permute-start(f32[144,256]{1,0:T(8,128)S(1)} %multiply_add_fusion.d0_ref), channel_id=1, source_target_pairs={{0,96},{32,0},{64,32},{96,64},{1,97},{33,1},{65,33},{97,65},{2,98}... | collective-permute-start | bytes 442376 | tf_op jit(solution)/shard_map/ppermute | solution.py:228
  (18 other events, 21.3 us)

commit v2 on v1

--- a/solution.py
+++ b/solution.py
@@ -23,6 +23,31 @@
     devices = range(lax.axis_size(axis))
     route = [(i - distance, i) for i in devices if i - distance in devices]
     return lax.ppermute(block, axis, route)
+
+
+def halo_copy_kernel(halo, t_hbm, m_hbm, tb_o, mb_o, ta_o, ma_o, sems):
+    depth = t_hbm.shape[0]
+    copies = [pltpu.make_async_copy(t_hbm.at[pl.ds(depth - halo, halo)], tb_o, sems.at[0]),
+              pltpu.make_async_copy(m_hbm.at[pl.ds(depth - halo, halo)], mb_o, sems.at[1]),
+              pltpu.make_async_copy(t_hbm.at[pl.ds(0, halo)], ta_o, sems.at[2]),
+              pltpu.make_async_copy(m_hbm.at[pl.ds(0, halo)], ma_o, sems.at[3])]
+    for c in copies:
+        c.start()
+    for c in copies:
+        c.wait()
+
+
+def halo_slices(temp, mat):
+    shape = (HALO,) + temp.shape[1:]
+    anyspec = pl.BlockSpec(memory_space=pl.ANY)
+    return pl.pallas_call(
+        functools.partial(halo_copy_kernel, HALO),
+        out_shape=[jax.ShapeDtypeStruct(shape, temp.dtype), jax.ShapeDtypeStruct(shape, mat.dtype)] * 2,
+        in_specs=[anyspec, anyspec],
+        out_specs=[anyspec] * 4,
+        scratch_shapes=[pltpu.SemaphoreType.DMA((4,))],
+        interpret=INTERPRET,
+    )(temp, mat)
 
 
 def harm(a, b):
@@ -182,10 +207,11 @@
     first_layer = g * local_depth
     ye = PAD_Y + strip + HALO + (-(PAD_Y + strip + HALO)) % 8
 
-    tb = from_behind(temp_start[local_depth - HALO:], "depth", 1)
-    mb = from_behind(cells_mat[local_depth - HALO:], "depth", 1)
-    ta = from_behind(temp_start[:HALO], "depth", -1)
-    ma = from_behind(cells_mat[:HALO], "depth", -1)
+    top_t, top_m, bottom_t, bottom_m = halo_slices(temp_start, cells_mat)
+    tb = from_behind(top_t, "depth", 1)
+    mb = from_behind(top_m, "depth", 1)
+    ta = from_behind(bottom_t, "depth", -1)
+    ma = from_behind(bottom_m, "depth", -1)
 
     def cols(sl):
         parts = [temp_start[:, :, sl], cells_mat[:, :, sl].astype(jnp.float32),

time: 106 us -> 205 us (1.93)
  the two profiles are of different devices: /device:TPU:25 before, /device:TPU:56 now
where the time goes in v2:
time: 205 us; the launch traced here: 202 us
  Pallas kernels  124 us (60%)
  waiting for transfers between devices  27.1 us (13%)
  starting transfers between devices  25.6 us (12%)
  local copies, waits for them, and re-layouts  17.9 us (9%)
  other arithmetic  3.71 us (2%)
  between operations  3.59 us (2%)
    pallas_call x1, Pallas kernels, halo_slices(): pl.pallas_call(functools.partial(halo_copy_kernel, HALO), out_shape=[jax....  96.4 us
    pallas_call x1, Pallas kernels, local_body(): pl.pallas_call(kern, out_shape=jax.ShapeDtypeStruct((local_depth, nx, str...  27.6 us
    ppermute x8, starting transfers between devices, from_behind(): return lax.ppermute(block, axis, route)  22.9 us
    ppermute x8, waiting for transfers between devices, from_behind(): return lax.ppermute(block, axis, route)  16 us
    ppermute x3, waiting for transfers between devices, local_body(): slots.append(lax.ppermute(power_w, 'depth', route))  11 us
    unnamed x51, local copies, waits for them, and re-layouts  8.83 us
    concatenate x6, local copies, waits for them, and re-layouts, widen(): jnp.concatenate([jnp.zeros((PAD_Y - HALO, nx), jnp.float32), lo, centre,...  5.77 us
  transfers between devices with their start and end apart: 14, of which 5 were waited for; matrix products, arithmetic and copies ran while one was open for 5% of the time, Pallas kernels for 48%

profile of v2, /device:TPU:56, one launch (start us, length us, event | category | flops | bytes accessed | tf_op | source)
XLA Modules:
  0.0 201.9 jit_solution(6513092669003307510)
XLA Ops:
  0.6 1.0 copy.13
  1.8 1.6 copy.9
  4.5 0.9 maximum_bitcast_fusion.1
  5.5 7.3 %collective-permute-start.5 = (f32[18,6,256]{2,1,0:T(8,128)S(1)}, f32[18,6,256]{2,1,0:T(8,128)S(1)}, u32[]{:S(2)}, u32[]{:S(2)}) collective-permute-start(f32[18,6,256]{2,1,0:T(8,128)S(1)} %maximum_bitcast_fusion.1), channel_id=1, source_target_pairs={{1,0},{2,1},{3,2},{4,3},{5,4},{6,5},{7,6},{8,7},{9,8},{10,9},{11,1... | collective-permute-start | bytes 331784 | tf_op jit(solution)/shard_map/ppermute | solution.py:25
  12.8 1.9 collective-permute-start.4
  18.9 5.6 %collective-permute-done.4.ylo_ref = f32[18,6,256]{2,1,0:T(8,128)S(1)} collective-permute-done((f32[18,6,256]{2,1,0:T(8,128)S(1)}, f32[18,6,256]{2,1,0:T(8,128)S(1)}, u32[]{:S(2)}, u32[]{:S(2)}) %collective-permute-start.4) | collective-permute-done | bytes 110624 | tf_op jit(solution)/shard_map/ppermute | solution.py:25
  24.7 1.1 collective-permute-start.9
  25.8 1.5 collective-permute-start.10
  29.1 1.9 collective-permute-start.6
  31.0 96.4 %shard_map.86 = (f32[6,256,128]{2,1,0:T(8,128)}, s32[6,256,128]{2,1,0:T(8,128)}, f32[6,256,128]{2,1,0:T(8,128)}, s32[6,256,128]{2,1,0:T(8,128)}) custom-call(f32[8,256,128]{2,1,0:T(8,128)} %bitcast.73, s32[8,256,128]{2,1,0:T(8,128)} %bitcast.75), custom_call_target="tpu_custom_call" | custom-call | tf_op jit(solution)/shard_map/pallas_call | solution.py:43
  127.4 1.9 collective-permute-start
  130.0 1.9 collective-permute-start.1
  132.6 3.6 %collective-permute-start.2 = (f32[6,256,128]{2,1,0:T(8,128)}, f32[6,256,128]{2,1,0:T(8,128)S(1)}, u32[]{:S(2)}, u32[]{:S(2)}) collective-permute-start(f32[6,256,128]{2,1,0:T(8,128)} %get-tuple-element.8), channel_id=1, source_target_pairs={{32,0},{64,32},{96,64},{33,1},{65,33},{97,65},{34,2},{66,34},{98,6... | collective-permute-start | bytes 2359304 | tf_op jit(solution)/shard_map/ppermute | solution.py:25
  136.3 2.5 %collective-permute-start.3 = (s32[6,256,128]{2,1,0:T(8,128)}, s32[6,256,128]{2,1,0:T(8,128)S(1)}, u32[]{:S(2)}, u32[]{:S(2)}) collective-permute-start(s32[6,256,128]{2,1,0:T(8,128)} %get-tuple-element.9), channel_id=1, source_target_pairs={{32,0},{64,32},{96,64},{33,1},{65,33},{97,65},{34,2},{66,34},{98,6... | collective-permute-start | bytes 2359304 | tf_op jit(solution)/shard_map/ppermute | solution.py:25
  138.9 1.9 concatenate.36
  140.8 1.9 concatenate.35
  142.6 1.9 concatenate.34
  144.5 1.9 collective-permute-start.7
  146.5 1.3 multiply_add_fusion.d0_ref
  147.7 10.4 %collective-permute-done.7.ca_ref = f32[2,6,12,256]{3,2,1,0:T(8,128)S(1)} collective-permute-done((f32[2,6,12,256]{3,2,1,0:T(8,128)}, f32[2,6,12,256]{3,2,1,0:T(8,128)S(1)}, u32[]{:S(2)}, u32[]{:S(2)}) %collective-permute-start.7) | collective-permute-done | bytes 147488 | tf_op jit(solution)/shard_map/ppermute | solution.py:25
  158.2 4.6 %collective-permute-done.11.d1_ref = f32[144,256]{1,0:T(8,128)S(1)} collective-permute-done((f32[144,256]{1,0:T(8,128)S(1)}, f32[144,256]{1,0:T(8,128)S(1)}, u32[]{:S(2)}, u32[]{:S(2)}) %collective-permute-start.11) | collective-permute-done | bytes 147488 | tf_op jit(solution)/shard_map/ppermute | solution.py:254
  164.1 4.5 %collective-permute-done.12.d2_ref = f32[144,256]{1,0:T(8,128)S(1)} collective-permute-done((f32[144,256]{1,0:T(8,128)S(1)}, f32[144,256]{1,0:T(8,128)S(1)}, u32[]{:S(2)}, u32[]{:S(2)}) %collective-permute-start.12) | collective-permute-done | bytes 147488 | tf_op jit(solution)/shard_map/ppermute | solution.py:254
  170.0 1.9 collective-permute-done.13.d3_ref
  174.3 27.6 %shard_map.87 = f32[8,256,128]{2,1,0:T(8,128)} custom-call(s32[6]{0:T(128)} %pad_add_fusion.sc_ref, f32[8]{0:T(128)} %ctab_ref.1, f32[8]{0:T(128)} %htab_ref.1, f32[8,256,128]{2,1,0:T(8,128)} %bitcast.74, s32[8,256,128]{2,1,0:T(8,128)} %bitcast.76, f32[6,256,128]{2,1,0:T(8,128)} %copy-done.3, s32[6,256,128]{2,1,0:T(8,128)} %copy-done.4, ...), custom_call_target="tpu_custom_call" | custom-call | tf_op jit(solution)/shard_map/pallas_call | solution.py:262
  (87 shorter events, 11.2 us)
Async XLA Ops:
  1.7 2.8 %copy-start.9 = (f32[1,1,256,128]{2,3,1,0:T(8,128)}, f32[1,1,256,128]{2,3,1,0:T(8,128)S(1)}, u32[]{:S(2)}) copy-start(f32[1,1,256,128]{2,3,1,0:T(8,128)S(1)} %copy.13) | copy-start | bytes 393220
  1.8 2.7 %copy-start.11 = (f32[1,1,256,128]{2,3,1,0:T(8,128)}, f32[1,1,256,128]{2,3,1,0:T(8,128)S(1)}, u32[]{:S(2)}) copy-start(f32[1,1,256,128]{2,3,1,0:T(8,128)S(1)} %copy.14) | copy-start | bytes 393220
  4.1 10.6 %copy-start.22 = (s32[4]{0:T(128)S(1)}, s32[4]{0:T(128)}, u32[]{:S(2)}) copy-start(s32[4]{0:T(128)} %param.13) | copy-start | bytes 52
  4.5 13.3 %copy-start = (f32[8,1,256,128]{3,2,1,0:T(8,128)S(1)}, f32[8,1,256,128]{3,2,1,0:T(8,128)}, u32[]{:S(2)}) copy-start(f32[8,1,256,128]{3,2,1,0:T(8,128)} %param.7) | copy-start | bytes 3145732
  5.5 13.4 %collective-permute-start.5 = (f32[18,6,256]{2,1,0:T(8,128)S(1)}, f32[18,6,256]{2,1,0:T(8,128)S(1)}, u32[]{:S(2)}, u32[]{:S(2)}) collective-permute-start(f32[18,6,256]{2,1,0:T(8,128)S(1)} %maximum_bitcast_fusion.1), channel_id=1, source_target_pairs={{1,0},{2,1},{3,2},{4,3},{5,4},{6,5},{7,6},{8,7},{9,8},{10,9},{11,1... | collective-permute-start | bytes 331784 | tf_op jit(solution)/shard_map/ppermute | solution.py:25
  12.8 11.7 %collective-permute-start.4 = (f32[18,6,256]{2,1,0:T(8,128)S(1)}, f32[18,6,256]{2,1,0:T(8,128)S(1)}, u32[]{:S(2)}, u32[]{:S(2)}) collective-permute-start(f32[18,6,256]{2,1,0:T(8,128)S(1)} %maximum_bitcast_fusion), channel_id=1, source_target_pairs={{0,1},{1,2},{2,3},{3,4},{4,5},{5,6},{6,7},{7,8},{8,9},{9,10},{10,1... | collective-permute-start | bytes 331784 | tf_op jit(solution)/shard_map/ppermute | solution.py:25
  18.8 8.5 %copy-start.7 = (f32[18,6,256]{2,1,0:T(8,128)}, f32[18,6,256]{2,1,0:T(8,128)S(1)}, u32[]{:S(2)}) copy-start(f32[18,6,256]{2,1,0:T(8,128)S(1)} %collective-permute-done.5.yhi_ref) | copy-start | bytes 331780
  24.5 2.9 %copy-start.8 = (f32[18,6,256]{2,1,0:T(8,128)}, f32[18,6,256]{2,1,0:T(8,128)S(1)}, u32[]{:S(2)}) copy-start(f32[18,6,256]{2,1,0:T(8,128)S(1)} %collective-permute-done.4.ylo_ref) | copy-start | bytes 331780
  24.6 104.8 %collective-permute-start.8 = (f32[144,256]{1,0:T(8,128)S(1)}, f32[144,256]{1,0:T(8,128)S(1)}, u32[]{:S(2)}, u32[]{:S(2)}) collective-permute-start(f32[144,256]{1,0:T(8,128)S(1)} %broadcast_select_fusion.2), channel_id=1, source_target_pairs={{0,32},{32,64},{64,96},{96,0},{1,33},{33,65},{65,97},{97,1},{2,34}... | collective-permute-start | bytes 442376 | tf_op jit(solution)/shard_map/ppermute | solution.py:245
  24.7 107.3 %collective-permute-start.9 = (f32[144,256]{1,0:T(8,128)S(1)}, f32[144,256]{1,0:T(8,128)S(1)}, u32[]{:S(2)}, u32[]{:S(2)}) collective-permute-start(f32[144,256]{1,0:T(8,128)S(1)} %broadcast_select_fusion.1), channel_id=1, source_target_pairs={{0,64},{32,96},{64,0},{96,32},{1,65},{33,97},{65,1},{97,33},{2,66}... | collective-permute-start | bytes 442376 | tf_op jit(solution)/shard_map/ppermute | solution.py:245
  25.8 110.4 %collective-permute-start.10 = (f32[144,256]{1,0:T(8,128)S(1)}, f32[144,256]{1,0:T(8,128)S(1)}, u32[]{:S(2)}, u32[]{:S(2)}) collective-permute-start(f32[144,256]{1,0:T(8,128)S(1)} %broadcast_select_fusion), channel_id=1, source_target_pairs={{0,96},{32,0},{64,32},{96,64},{1,97},{33,1},{65,33},{97,65},{2,98}... | collective-permute-start | bytes 442376 | tf_op jit(solution)/shard_map/ppermute | solution.py:245
  29.1 115.5 %collective-permute-start.6 = (f32[2,6,12,256]{3,2,1,0:T(8,128)}, f32[2,6,12,256]{3,2,1,0:T(8,128)}, u32[]{:S(2)}, u32[]{:S(2)}) collective-permute-start(f32[2,6,12,256]{3,2,1,0:T(8,128)} %get-tuple-element.21), channel_id=1, source_target_pairs={{0,32},{32,64},{64,96},{1,33},{33,65},{65,97},{2,34},{34,66},{66,9... | collective-permute-start | bytes 442376 | tf_op jit(solution)/shard_map/ppermute | solution.py:25
  31.0 107.8 %copy-start.14 = (f32[1,1,256,128]{3,2,1,0:T(8,128)S(1)}, f32[1,1,256,128]{3,2,1,0:T(8,128)}, u32[]{:S(2)}) copy-start(f32[1,1,256,128]{3,2,1,0:T(8,128)} %get-tuple-element.12) | copy-start | bytes 393220
  127.4 44.5 %collective-permute-start = (f32[6,256,128]{2,1,0:T(8,128)}, f32[6,256,128]{2,1,0:T(8,128)S(1)}, u32[]{:S(2)}, u32[]{:S(2)}) collective-permute-start(f32[6,256,128]{2,1,0:T(8,128)} %get-tuple-element.6), channel_id=1, source_target_pairs={{0,32},{32,64},{64,96},{1,33},{33,65},{65,97},{2,34},{34,66},{66,9... | collective-permute-start | bytes 2359304 | tf_op jit(solution)/shard_map/ppermute | solution.py:25
  130.0 41.9 %collective-permute-start.1 = (s32[6,256,128]{2,1,0:T(8,128)}, s32[6,256,128]{2,1,0:T(8,128)S(1)}, u32[]{:S(2)}, u32[]{:S(2)}) collective-permute-start(s32[6,256,128]{2,1,0:T(8,128)} %get-tuple-element.7), channel_id=1, source_target_pairs={{0,32},{32,64},{64,96},{1,33},{33,65},{65,97},{2,34},{34,66},{66,9... | collective-permute-start | bytes 2359304 | tf_op jit(solution)/shard_map/ppermute | solution.py:25
  132.6 39.4 %collective-permute-start.2 = (f32[6,256,128]{2,1,0:T(8,128)}, f32[6,256,128]{2,1,0:T(8,128)S(1)}, u32[]{:S(2)}, u32[]{:S(2)}) collective-permute-start(f32[6,256,128]{2,1,0:T(8,128)} %get-tuple-element.8), channel_id=1, source_target_pairs={{32,0},{64,32},{96,64},{33,1},{65,33},{97,65},{34,2},{66,34},{98,6... | collective-permute-start | bytes 2359304 | tf_op jit(solution)/shard_map/ppermute | solution.py:25
  136.3 35.7 %collective-permute-start.3 = (s32[6,256,128]{2,1,0:T(8,128)}, s32[6,256,128]{2,1,0:T(8,128)S(1)}, u32[]{:S(2)}, u32[]{:S(2)}) collective-permute-start(s32[6,256,128]{2,1,0:T(8,128)} %get-tuple-element.9), channel_id=1, source_target_pairs={{32,0},{64,32},{96,64},{33,1},{65,33},{97,65},{34,2},{66,34},{98,6... | collective-permute-start | bytes 2359304 | tf_op jit(solution)/shard_map/ppermute | solution.py:25
  142.6 3.8 %copy-start.13 = (f32[144,256]{1,0:T(8,128)S(1)}, f32[144,256]{1,0:T(8,128)}, u32[]{:S(2)}) copy-start(f32[144,256]{1,0:T(8,128)} %concatenate.36) | copy-start | bytes 442372
  144.5 13.6 %collective-permute-start.7 = (f32[2,6,12,256]{3,2,1,0:T(8,128)}, f32[2,6,12,256]{3,2,1,0:T(8,128)S(1)}, u32[]{:S(2)}, u32[]{:S(2)}) collective-permute-start(f32[2,6,12,256]{3,2,1,0:T(8,128)} %get-tuple-element.20), channel_id=1, source_target_pairs={{32,0},{64,32},{96,64},{33,1},{65,33},{97,65},{34,2},{66,34},{98,6... | collective-permute-start | bytes 442376 | tf_op jit(solution)/shard_map/ppermute | solution.py:25
  147.7 22.3 %copy-start.2 = (f32[144,256]{1,0:T(8,128)}, f32[144,256]{1,0:T(8,128)S(1)}, u32[]{:S(2)}) copy-start(f32[144,256]{1,0:T(8,128)S(1)} %multiply_add_fusion.d0_ref) | copy-start | bytes 442372
  158.2 4.6 %copy-start.15 = (f32[2,6,12,256]{3,2,1,0:T(8,128)}, f32[2,6,12,256]{3,2,1,0:T(8,128)S(1)}, u32[]{:S(2)}) copy-start(f32[2,6,12,256]{3,2,1,0:T(8,128)S(1)} %collective-permute-done.7.ca_ref) | copy-start | bytes 442372
  158.2 4.6 %collective-permute-start.11 = (f32[144,256]{1,0:T(8,128)S(1)}, f32[144,256]{1,0:T(8,128)S(1)}, u32[]{:S(2)}, u32[]{:S(2)}) collective-permute-start(f32[144,256]{1,0:T(8,128)S(1)} %multiply_add_fusion.d0_ref), channel_id=1, source_target_pairs={{0,32},{32,64},{64,96},{96,0},{1,33},{33,65},{65,97},{97,1},{2,34}... | collective-permute-start | bytes 442376 | tf_op jit(solution)/shard_map/ppermute | solution.py:254
  163.5 5.1 %collective-permute-start.12 = (f32[144,256]{1,0:T(8,128)S(1)}, f32[144,256]{1,0:T(8,128)S(1)}, u32[]{:S(2)}, u32[]{:S(2)}) collective-permute-start(f32[144,256]{1,0:T(8,128)S(1)} %multiply_add_fusion.d0_ref), channel_id=1, source_target_pairs={{0,64},{32,96},{64,0},{96,32},{1,65},{33,97},{65,1},{97,33},{2,66}... | collective-permute-start | bytes 442376 | tf_op jit(solution)/shard_map/ppermute | solution.py:254
  169.3 2.7 %collective-permute-start.13 = (f32[144,256]{1,0:T(8,128)S(1)}, f32[144,256]{1,0:T(8,128)}, u32[]{:S(2)}, u32[]{:S(2)}) collective-permute-start(f32[144,256]{1,0:T(8,128)S(1)} %multiply_add_fusion.d0_ref), channel_id=1, source_target_pairs={{0,96},{32,0},{64,32},{96,64},{1,97},{33,1},{65,33},{97,65},{2,98}... | collective-permute-start | bytes 442376 | tf_op jit(solution)/shard_map/ppermute | solution.py:254
  (14 other events, 17.5 us)
